TPU v7x, 32 devices: a whole 2x2x4 slice. The times are simulated.
32 devices in a mesh: ctx: 8 (over z, x), probe: 4 (over y, core).
Axes of the slice: x: 2, y: 2, z: 4, core: 2. Of those that a mesh axis runs over, the one named last changes fastest.
Arguments:
- features: float32 [3, 2048, 1024], P(None, 'ctx'), may hold values from -6 to 6
- cotangent: float32 [2048, 1024], P('ctx'), may hold values from -48 to 48
- gate_logits: float32 [4], replicated, may hold values from -4 to 4
- probes: int32 [4, 3, 2048, 1024], P('probe', None, 'ctx'), may hold values from -1 to 1, as said below
Outputs:
- products: float32 [4, 3, 2048, 1024], P('probe', None, 'ctx')
- block_trace: float32 [8, 3, 4], P('ctx')
Inputs may be any that keep to these rules, and one draw needn't show every extreme that they name: `probes`: every entry is -1 or 1.
All inputs are finite; a program needn't handle non-finite values.
Results may differ from a plain program's by a relative error of at most 0.0003.
Values sent between devices are 32-bit elements; how exact they have to be, the bound alone decides.
No kernel may reach another device: no remote copies, remote signals or barrier semaphores. Data moves between devices by JAX's collectives and lax.ppermute only.
A program may use at most 192 MiB of HBM per device.

v0:
```python
import jax
import jax.numpy as jnp
from jax import lax
from jax.sharding import PartitionSpec as P

HIGHEST = lax.Precision.HIGHEST


def entering(part, axis, combine, identity, reverse):
    count = lax.axis_size(axis)
    place = lax.axis_index(axis)
    ahead = count - 1 - place if reverse else place
    gathered = jax.tree.map(lambda a: lax.all_gather(a, axis), part)
    state = jax.tree.map(lambda a, e: jnp.zeros_like(a) + jnp.asarray(e, a.dtype), part, identity)

    def one(turn, state):
        source = count - 1 - turn if reverse else turn
        return combine(
            state, jax.tree.map(lambda a: lax.dynamic_index_in_dim(a, source, 0, False), gathered)
        )

    return lax.fori_loop(0, ahead, one, state)


def feature_map(inputs):
    return jnp.where(inputs > 0, inputs + 1.0, jnp.exp(jnp.minimum(inputs, 0.0)))


def feature_slope(inputs):
    return jnp.where(inputs > 0, 1.0, jnp.exp(jnp.minimum(inputs, 0.0)))


def feature_curve(inputs):
    return jnp.where(inputs > 0, 0.0, jnp.exp(jnp.minimum(inputs, 0.0)))


def segment_loss(query_rows, key_rows, value_rows, memory, normalizer, cot_rows, gate_logits):
    query_feat = feature_map(query_rows)
    retrieved = jnp.einsum("sha,hab->shb", query_feat, memory, precision=HIGHEST)
    denom_mem = jnp.einsum("sha,ha->sh", query_feat, normalizer, precision=HIGHEST) + 1.0
    from_memory = retrieved / denom_mem[:, :, None]
    seg_rows = query_rows.shape[0]
    scale = query_rows.shape[-1] ** (-0.5)
    causal = lax.broadcasted_iota(jnp.int32, (seg_rows, seg_rows), 0) >= lax.broadcasted_iota(
        jnp.int32, (seg_rows, seg_rows), 1
    )
    logits = jnp.einsum("sha,tha->hst", query_rows, key_rows, precision=HIGHEST) * scale
    logits = jnp.where(causal[None], logits, -1e30)
    top = lax.stop_gradient(jnp.max(logits, axis=2, keepdims=True))
    weights = jnp.exp(logits - top)
    local_num = jnp.einsum("hst,thb->shb", weights, value_rows, precision=HIGHEST)
    local_den = jnp.transpose(jnp.sum(weights, axis=2))
    from_local = local_num / local_den[:, :, None]
    mixing = jax.nn.sigmoid(gate_logits)[None, :, None]
    output = mixing * from_memory + (1.0 - mixing) * from_local
    return jnp.sum(cot_rows * output)


def add_trees(earlier, later):
    return jax.tree.map(jnp.add, earlier, later)


def shards(features, cotangent, gate_logits, probes):
    heads = gate_logits.shape[0]
    seg_rows = features.shape[1]
    head_size = features.shape[2] // heads
    shaped = features.reshape(3, seg_rows, heads, head_size)
    query_rows, key_rows, value_rows = (shaped[0], shaped[1], shaped[2])
    cot_rows = cotangent.reshape(seg_rows, heads, head_size)
    signs = probes[0].astype(jnp.float32).reshape(3, seg_rows, heads, head_size)
    query_dir, key_dir, value_dir = (signs[0], signs[1], signs[2])
    key_feat = feature_map(key_rows)
    key_slope = feature_slope(key_rows)
    key_tan = key_slope * key_dir
    increment = jnp.einsum("sha,shb->hab", key_feat, value_rows, precision=HIGHEST)
    norm_inc = jnp.sum(key_feat, axis=0)
    increment_tan = jnp.einsum("sha,shb->hab", key_tan, value_rows, precision=HIGHEST) + jnp.einsum(
        "sha,shb->hab", key_feat, value_dir, precision=HIGHEST
    )
    norm_tan = jnp.sum(key_tan, axis=0)
    groups = lax.axis_size("probe")
    share = heads // groups
    first_head = lax.axis_index("probe") * share
    zero_mem = jnp.zeros((heads, head_size, head_size), jnp.float32)
    zero_norm = jnp.zeros((heads, head_size), jnp.float32)
    zero_share = jnp.zeros((share, head_size, head_size), jnp.float32)
    own_inc = lax.dynamic_slice_in_dim(increment, first_head, share, 0)
    own_prefix, normalizer, memory_tan, normalizer_tan = entering(
        (own_inc, norm_inc, increment_tan, norm_tan),
        "ctx",
        add_trees,
        (zero_share, zero_norm, zero_mem, zero_norm),
        False,
    )
    memory = lax.all_gather(own_prefix, "probe", axis=0, tiled=True)

    def local_loss(point):
        return segment_loss(point[0], point[1], point[2], point[3], point[4], cot_rows, gate_logits)

    point = (query_rows, key_rows, value_rows, memory, normalizer)
    grads, pullback = jax.vjp(jax.grad(local_loss), point)
    curvature = pullback((query_dir, key_dir, value_dir, memory_tan, normalizer_tan))[0]
    own_back = lax.dynamic_slice_in_dim(grads[3], first_head, share, 0)
    own_suffix, back_norm, back_mem_tan, back_norm_tan = entering(
        (own_back, grads[4], curvature[3], curvature[4]),
        "ctx",
        add_trees,
        (zero_share, zero_norm, zero_mem, zero_norm),
        True,
    )
    back_mem = lax.all_gather(own_suffix, "probe", axis=0, tiled=True)
    through = jnp.einsum("shb,hab->sha", value_rows, back_mem, precision=HIGHEST) + back_norm[None]
    through_tan = (
        jnp.einsum("shb,hab->sha", value_dir, back_mem, precision=HIGHEST)
        + jnp.einsum("shb,hab->sha", value_rows, back_mem_tan, precision=HIGHEST)
        + back_norm_tan[None]
    )
    key_out = curvature[1] + feature_curve(key_rows) * key_dir * through + key_slope * through_tan
    value_out = (
        curvature[2]
        + jnp.einsum("sha,hab->shb", key_tan, back_mem, precision=HIGHEST)
        + jnp.einsum("sha,hab->shb", key_feat, back_mem_tan, precision=HIGHEST)
    )
    stacked = jnp.stack((curvature[0], key_out, value_out))
    products = stacked.reshape(1, 3, seg_rows, heads * head_size)
    partial_trace = jnp.sum(signs * stacked, axis=(1, 3)) / (seg_rows * groups)
    block_trace = lax.psum(partial_trace, "probe")
    return (products, block_trace.reshape(1, 3, heads))


def solution(mesh):
    placed = (P(None, "ctx", None), P("ctx", None), P(), P("probe", None, "ctx", None))
    return jax.shard_map(
        shards,
        mesh=mesh,
        in_specs=placed,
        out_specs=(P("probe", None, "ctx", None), P("ctx", None, None)),
        check_vma=False,
    )
```

profile of v0, /device:TPU:0, one launch (start us, length us, event | category | flops | bytes accessed | tf_op | source)
XLA Modules:
  0.0 484.1 jit_solution(11972801363494513276)
XLA Ops:
  7.2 3.1 fusion.134
  13.2 3.5 copy.177
  16.8 2.1 convert_element_type.6
  22.3 2.4 convolution_add_fusion.7
  24.8 1.7 fusion.52
  28.1 2.6 copy.179
  30.6 32.7 %all_gather.57 = f32[8,4,256]{2,1,0:T(4,128)S(1)} all-gather(f32[1,4,256]{2,1,0:T(4,128)S(1)} %all_gather.56), channel_id=1, replica_groups=mesh['ctx'=8,'probe'=4] {'ctx'}, dimensions={0}, use_global_device_ids=true | all-gather | bytes 36864 | tf_op jit(solution)/shard_map/all_gather | solution.py:13
  63.3 31.3 %all_gather.61 = f32[8,4,256]{2,1,0:T(4,128)S(1)} all-gather(f32[1,4,256]{2,1,0:T(4,128)S(1)} %all_gather.60), channel_id=1, replica_groups=mesh['ctx'=8,'probe'=4] {'ctx'}, dimensions={0}, use_global_device_ids=true | all-gather | bytes 36864 | tf_op jit(solution)/shard_map/all_gather | solution.py:13
  94.6 1.9 fusion.23
  97.1 1.9 fusion.55
  99.0 3.0 multiply_reduce_fusion.5
  104.0 87.6 %all-gather.21.cloned.1.call-done = f32[32,256,256]{2,1,0:T(8,128)} async-done(((f32[4,256,256]{2,1,0:T(8,128)}), f32[32,256,256]{2,1,0:T(8,128)}) %all-gather.21.cloned.1.call-update) | async-done | bytes 8388624 | tf_op jit(solution)/shard_map/all_gather | solution.py:13
  196.2 1.9 fusion.44
  198.9 2.9 fusion.132
  201.8 23.2 %all-gather.15.cloned.1.call-done = f32[4,256,256]{2,1,0:T(8,128)} async-done(((f32[1,256,256]{2,1,0:T(8,128)}), f32[4,256,256]{2,1,0:T(8,128)}) %all-gather.15.cloned.1.call-update) | async-done | bytes 1048592 | tf_op jit(solution)/shard_map/all_gather | solution.py:95
  225.1 3.3 convolution_bitcast_fusion.5
  228.5 1.7 multiply_reduce_fusion.3
  230.3 2.0 fusion.36
  234.8 2.5 fusion.42
  237.3 2.6 convolution_add_fusion.2
  240.0 2.8 fusion.135
  245.5 2.3 fusion.2
  251.0 30.9 %all-gather.7 = f32[8,4,256]{2,1,0:T(4,128)S(1)} all-gather(f32[1,4,256]{2,1,0:T(4,128)S(1)} %fusion.102), channel_id=7, replica_groups=mesh['ctx'=8,'probe'=4] {'ctx'}, dimensions={0}, use_global_device_ids=true | all-gather | bytes 36864 | tf_op jit(solution)/shard_map/all_gather | solution.py:13
  281.9 31.1 %all-gather.6 = f32[8,4,256]{2,1,0:T(4,128)S(1)} all-gather(f32[1,4,256]{2,1,0:T(4,128)S(1)} %bitcast.357), channel_id=5, replica_groups=mesh['ctx'=8,'probe'=4] {'ctx'}, dimensions={0}, use_global_device_ids=true | all-gather | bytes 36864 | tf_op jit(solution)/shard_map/all_gather | solution.py:13
  313.0 2.1 convolution_add_fusion.13
  315.1 2.4 fusion.15
  317.5 2.3 fusion.90
  319.8 2.3 fusion.89
  322.2 3.1 fusion.21
  325.3 84.8 %all-gather.25.cloned.1.call-done = f32[32,256,256]{2,1,0:T(8,128)} async-done(((f32[4,256,256]{2,1,0:T(8,128)}), f32[32,256,256]{2,1,0:T(8,128)}) %all-gather.25.cloned.1.call-update) | async-done | bytes 8388624 | tf_op jit(solution)/shard_map/all_gather | solution.py:13
  411.2 26.5 %while.35 = (s32[]{:T(128)}, f32[1,256,256]{2,1,0:T(8,128)S(1)}, f32[4,256]{1,0:T(4,128)S(1)}, f32[4,256,256]{2,1,0:T(8,128)}, f32[4,256]{1,0:T(4,128)S(1)}, /*i...) while((s32[]{:T(128)}, f32[1,256,256]{2,1,0:T(8,128)S(1)}, ...), condition=%wide.region_14.15_spmd, body=%wide.region_13.14_spmd.sunk | while | flops 329734 | bytes 3956927 | solution.py:22
  411.2 2.7 bitcast_add_fusion.22
  415.0 2.7 bitcast_add_fusion.22
  418.7 2.7 bitcast_add_fusion.22
  422.4 2.7 bitcast_add_fusion.22
  426.1 2.7 bitcast_add_fusion.22
  429.9 2.7 bitcast_add_fusion.22
  433.6 2.7 bitcast_add_fusion.22
  438.5 3.1 fusion.11
  441.7 2.2 fusion.27
  443.9 1.9 fusion.35
  445.9 2.3 fusion.28
  448.2 4.3 all-gather.17.cloned.1.call-done
  452.6 3.8 fusion.1
  456.4 1.9 fusion
  464.9 2.1 multiply_reduce_fusion
  467.1 3.5 copy.216
  470.6 5.9 %psum.7 = f32[1,3,4]{2,1,0:T(4,128)S(1)} all-reduce(f32[1,3,4]{2,1,0:T(4,128)S(1)} %multiply_bitcast_fusion), channel_id=1, replica_groups=mesh['ctx'=8,'probe'=4] {'probe'}, use_global_device_ids=true, to_apply=%region_17.18 | all-reduce | flops 12 | bytes 96 | tf_op jit(solution)/shard_map/psum | solution.py:127
  (187 shorter events, 40.4 us)
Async XLA Ops:
  7.2 96.9 %all-gather.19.cloned.1.call-start = ((), (), s32[]{:S(2)}) async-start(), calls=%async_computation.2 | async-start | bytes 2359296 | tf_op jit(solution)/shard_map/all_gather | solution.py:13
  11.0 9.9 %copy-start.8 = (f32[1,256,1024]{1,2,0:T(8,128)}, f32[1,256,1024]{1,2,0:T(8,128)S(1)}, u32[]{:S(2)}) copy-start(f32[1,256,1024]{1,2,0:T(8,128)S(1)} %copy.172) | copy-start | bytes 3145732
  13.2 178.5 %all-gather.21.cloned.1.call-start = ((), (), s32[]{:S(2)}) async-start(), calls=%async_computation.3 | async-start | bytes 9437184 | tf_op jit(solution)/shard_map/all_gather | solution.py:13
  18.9 2.0 copy-start.20
  20.9 78.1 %copy-start.13 = (f32[1,1,256,1024]{2,3,1,0:T(8,128)}, f32[1,1,256,1024]{2,3,1,0:T(8,128)S(1)}, u32[]{:S(2)}) copy-start(f32[1,1,256,1024]{2,3,1,0:T(8,128)S(1)} %get-tuple-element.345) | copy-start | bytes 3145732
  24.7 200.3 %all-gather.15.cloned.1.call-start = ((), (), s32[]{:S(2)}) async-start(), calls=%async_computation | async-start | bytes 1310720 | tf_op jit(solution)/shard_map/all_gather | solution.py:95
  30.6 66.5 %copy-start.36 = (f32[256,4,256]{2,0,1:T(8,128)S(1)}, f32[256,4,256]{2,0,1:T(8,128)}, u32[]{:S(2)}) copy-start(f32[256,4,256]{2,0,1:T(8,128)} %copy.179) | copy-start | bytes 3145732
  97.1 4.9 %copy-start.1 = (f32[4,256,256]{1,2,0:T(8,128)}, f32[4,256,256]{1,2,0:T(8,128)S(1)}, u32[]{:S(2)}) copy-start(f32[4,256,256]{1,2,0:T(8,128)S(1)} %subtract_exponential_fusion) | copy-start | bytes 3145732
  99.0 3.6 copy-start.23
  102.0 143.5 %copy-start.40 = (f32[256,4]{0,1:T(4,128)}, f32[256,4]{0,1:T(4,128)S(1)}, u32[]{:S(2)}) copy-start(f32[256,4]{0,1:T(4,128)S(1)} %multiply_divide_fusion.3) | copy-start | bytes 12292
  192.5 132.7 %all-gather.23.cloned.1.call-start = ((), (), s32[]{:S(2)}) async-start(), calls=%async_computation.4 | async-start | bytes 2359296 | tf_op jit(solution)/shard_map/all_gather | solution.py:13
  193.8 121.3 %copy-start.49 = (f32[4]{0:T(128)}, f32[4]{0:T(128)S(1)}, u32[]{:S(2)}) copy-start(f32[4]{0:T(128)S(1)} %get-tuple-element.336) | copy-start | bytes 52
  193.8 128.4 %copy-start.47 = (f32[4]{0:T(128)}, f32[4]{0:T(128)S(1)}, u32[]{:S(2)}) copy-start(f32[4]{0:T(128)S(1)} %get-tuple-element.335) | copy-start | bytes 52
  195.4 3.5 copy-start.6
  196.2 41.1 %copy-start.42 = (f32[256,4]{0,1:T(4,128)}, f32[256,4]{0,1:T(4,128)S(1)}, u32[]{:S(2)}) copy-start(f32[256,4]{0,1:T(4,128)S(1)} %multiply_divide_fusion.2) | copy-start | bytes 12292
  198.9 38.4 %copy-start.44 = (f32[256,4]{0,1:T(4,128)}, f32[256,4]{0,1:T(4,128)S(1)}, u32[]{:S(2)}) copy-start(f32[256,4]{0,1:T(4,128)S(1)} %fusion.104) | copy-start | bytes 12292
  198.9 29.5 %copy-start.45 = (f32[256,4]{0,1:T(4,128)S(1)}, f32[256,4]{0,1:T(4,128)}, u32[]{:S(2)}) copy-start(f32[256,4]{0,1:T(4,128)} %negate_bitcast_fusion) | copy-start | bytes 12292
  225.1 3.4 copy-start.2
  225.1 3.4 copy-start.9
  232.3 82.8 %copy-start.51 = (f32[256,4]{0,1:T(4,128)}, f32[256,4]{0,1:T(4,128)S(1)}, u32[]{:S(2)}) copy-start(f32[256,4]{0,1:T(4,128)S(1)} %get-tuple-element.352) | copy-start | bytes 12292
  234.6 175.5 %all-gather.25.cloned.1.call-start = ((), (), s32[]{:S(2)}) async-start(), calls=%async_computation.5 | async-start | bytes 9437184 | tf_op jit(solution)/shard_map/all_gather | solution.py:13
  239.9 212.7 %all-gather.17.cloned.1.call-start = ((), (), s32[]{:S(2)}) async-start(), calls=%async_computation.1 | async-start | bytes 1310720 | tf_op jit(solution)/shard_map/all_gather | solution.py:111
  240.0 2.9 copy-start.3
  240.0 2.9 copy-start.10
  240.0 2.9 copy-start.33
  245.5 3.4 copy-start.22
  247.8 67.3 %copy-start.53 = (f32[4,256]{1,0:T(4,128)}, f32[4,256]{1,0:T(4,128)S(1)}, u32[]{:S(2)}) copy-start(f32[4,256]{1,0:T(4,128)S(1)} %get-tuple-element.349) | copy-start | bytes 12292
  249.9 65.2 %copy-start.7 = (f32[4,256,256]{2,1,0:T(8,128)S(1)}, f32[4,256,256]{2,1,0:T(8,128)}, u32[]{:S(2)}) copy-start(f32[4,256,256]{2,1,0:T(8,128)} %copy-done.5) | copy-start | bytes 3145732
  315.1 2.4 copy-start.14
  317.5 2.3 copy-start.24
  319.8 2.3 copy-start.18
  411.2 27.3 %copy-start.43 = (f32[256,4]{0,1:T(4,128)S(1)}, f32[256,4]{0,1:T(4,128)}, u32[]{:S(2)}) copy-start(f32[256,4]{0,1:T(4,128)} %copy-done.42) | copy-start | bytes 12292
  437.7 3.9 copy-start.41
  437.7 3.9 copy-start.46
  437.7 3.9 copy-start.48
  438.5 3.1 copy-start.4
  438.5 3.1 copy-start.11
  438.5 3.1 copy-start.39
  441.6 2.2 copy-start.25
  441.6 2.2 copy-start.29
  441.6 2.2 copy-start.50
  441.7 2.2 copy-start.52
  441.7 2.2 copy-start.54
  448.2 8.2 %copy-start = (f32[4,256,256]{2,1,0:T(8,128)S(1)}, f32[4,256,256]{2,1,0:T(8,128)}, u32[]{:S(2)}) copy-start(f32[4,256,256]{2,1,0:T(8,128)} %get-tuple-element.195) | copy-start | bytes 3145732
  456.4 2.0 copy-start.19
  456.4 2.0 copy-start.30
  456.4 3.1 copy-start.12
  462.7 2.2 copy-start.34
  (13 other events, 19.8 us)
Sparse Core Ops, SparseCore 0:
  13.3 52.4 all-gather.18
  67.9 123.7 all-gather.20
  193.2 31.8 all-gather.14
  234.7 49.8 all-gather.22
  286.5 123.4 all-gather.24
  438.6 13.9 all-gather.16
where the time goes:
time: 491 us; the launch traced here: 484 us
  waiting for transfers between devices  200 us (41%)
  blocking collectives  132 us (27%)
  matrix products  75.6 us (15%)
  other arithmetic  35.3 us (7%)
  local copies, waits for them, and re-layouts  24.5 us (5%)
  between operations  15.3 us (3%)
    all_gather x4, waiting for transfers between devices, entering(): gathered = jax.tree.map(lambda a: lax.all_gather(a, axis), part)  172 us
    all_gather x4, blocking collectives, entering(): gathered = jax.tree.map(lambda a: lax.all_gather(a, axis), part)  126 us
    add x21, other arithmetic, add_trees(): return jax.tree.map(jnp.add, earlier, later)  25.9 us
    all_gather x1, waiting for transfers between devices, shards(): memory = lax.all_gather(own_prefix, 'probe', axis=0, tiled=True)  23.2 us
    dot_general x9, matrix products, segment_loss(): jnp.einsum('sha,hab->shb', query_feat, memory, precision=HIGHEST)  22.2 us
    dot_general x8, matrix products, segment_loss(): jnp.einsum('hst,thb->shb', weights, value_rows, precision=HIGHEST)  16.8 us
    dot_general x7, matrix products, segment_loss(): jnp.einsum('sha,tha->hst', query_rows, key_rows, precision=HIGHEST) * scale  15 us
    unnamed x116, local copies, waits for them, and re-layouts  14.3 us
  transfers between devices with their start and end apart: 6, of which 4 were waited for; matrix products, arithmetic and copies ran while one was open for 15% of the time, Pallas kernels for 0%

commit v1 on v0

--- a/solution.py
+++ b/solution.py
@@ -92,7 +92,16 @@
         (zero_share, zero_norm, zero_mem, zero_norm),
         False,
     )
-    memory = lax.all_gather(own_prefix, "probe", axis=0, tiled=True)
+    ways = lax.axis_size("probe")
+    up = [(d, (d + 1) % ways) for d in range(ways)]
+    down = [(d, (d - 1) % ways) for d in range(ways)]
+    earlier_2, later_2 = ([own_prefix], [own_prefix])
+    for _ in range(ways // 2):
+        earlier_2.append(lax.ppermute(earlier_2[-1], "probe", up))
+    for _ in range((ways - 1) // 2):
+        later_2.append(lax.ppermute(later_2[-1], "probe", down))
+    line = jnp.concatenate([*earlier_2[::-1], *later_2[1:]], axis=0)
+    memory = jnp.roll(line, (lax.axis_index("probe") - ways // 2) * own_prefix.shape[0], axis=0)
 
     def local_loss(point):
         return segment_loss(point[0], point[1], point[2], point[3], point[4], cot_rows, gate_logits)

time: 491 us -> 495 us (level)
  blocking collectives: 132 us -> 154 us
  waiting for transfers between devices: 200 us -> 179 us
    all_gather x1 -> x0, waiting for transfers between devices: 23.2 us -> none  [shards(): memory = lax.all_gather(own_prefix, 'probe', axis=0, tiled=True)]
    all_gather x4, blocking collectives: 126 us -> 148 us  [entering(): gathered = jax.tree.map(lambda a: lax.all_gather(a, axis), part)]
    ppermute x0 -> x3, waiting for transfers between devices: none -> 5.74 us  [the longest x2 5.74 us: shards(): earlier_2.append(lax.ppermute(earlier_2[-1], 'probe', up))]
    unnamed x116 -> x135, local copies, waits for them, and re-layouts: 14.3 us -> 15.4 us
  transfers between devices with their start and end apart: 6 -> 8, of which waited for: 4 -> 4; matrix products, arithmetic and copies ran while one was open for 15% -> 15% of each run, Pallas kernels for 0% -> 0%
where the time goes in v1:
time: 495 us; the launch traced here: 488 us
  waiting for transfers between devices  179 us (36%)
  blocking collectives  154 us (31%)
  matrix products  75.2 us (15%)
  other arithmetic  35.7 us (7%)
  local copies, waits for them, and re-layouts  26.2 us (5%)
  between operations  15.3 us (3%)
    all_gather x4, waiting for transfers between devices, entering(): gathered = jax.tree.map(lambda a: lax.all_gather(a, axis), part)  173 us
    all_gather x4, blocking collectives, entering(): gathered = jax.tree.map(lambda a: lax.all_gather(a, axis), part)  148 us
    add x21, other arithmetic, add_trees(): return jax.tree.map(jnp.add, earlier, later)  25.8 us
    dot_general x9, matrix products, segment_loss(): jnp.einsum('sha,hab->shb', query_feat, memory, precision=HIGHEST)  22.7 us
    dot_general x8, matrix products, segment_loss(): jnp.einsum('hst,thb->shb', weights, value_rows, precision=HIGHEST)  17 us
    unnamed x135, local copies, waits for them, and re-layouts  15.4 us
    dot_general x7, matrix products, segment_loss(): jnp.einsum('sha,tha->hst', query_rows, key_rows, precision=HIGHEST) * scale  14 us
  transfers between devices with their start and end apart: 8, of which 4 were waited for; matrix products, arithmetic and copies ran while one was open for 15% of the time, Pallas kernels for 0%

profile of v1, /device:TPU:0, one launch (start us, length us, event | category | flops | bytes accessed | tf_op | source)
XLA Modules:
  0.0 488.0 jit_solution(14984807898409578619)
XLA Ops:
  7.2 3.1 fusion.141
  13.2 3.5 copy.187
  16.8 2.1 convert_element_type.6
  22.3 2.4 convolution_add_fusion.7
  24.8 1.8 fusion.51
  26.6 1.6 copy.283
  29.5 1.6 copy.177
  31.1 32.7 %all_gather.54 = f32[8,4,256]{2,1,0:T(4,128)S(1)} all-gather(f32[1,4,256]{2,1,0:T(4,128)S(1)} %all_gather.53), channel_id=1, replica_groups=mesh['ctx'=8,'probe'=4] {'ctx'}, dimensions={0}, use_global_device_ids=true | all-gather | bytes 36864 | tf_op jit(solution)/shard_map/all_gather | solution.py:13
  63.7 31.0 %all_gather.58 = f32[8,4,256]{2,1,0:T(4,128)S(1)} all-gather(f32[1,4,256]{2,1,0:T(4,128)S(1)} %all_gather.57), channel_id=1, replica_groups=mesh['ctx'=8,'probe'=4] {'ctx'}, dimensions={0}, use_global_device_ids=true | all-gather | bytes 36864 | tf_op jit(solution)/shard_map/all_gather | solution.py:13
  95.4 1.9 fusion.22
  97.9 1.9 fusion.54
  99.8 3.0 multiply_reduce_fusion.5
  105.4 2.1 convolution_bitcast_fusion.6
  107.6 83.8 %all-gather.18.cloned.1.call-done = f32[32,256,256]{2,1,0:T(8,128)} async-done(((f32[4,256,256]{2,1,0:T(8,128)}), f32[32,256,256]{2,1,0:T(8,128)}) %all-gather.18.cloned.1.call-update) | async-done | bytes 8388624 | tf_op jit(solution)/shard_map/all_gather | solution.py:13
  193.3 2.1 collective-permute-start.2
  195.5 2.1 fusion.117
  197.6 3.2 fusion.139
  202.3 5.7 %collective-permute-done.1 = f32[1,256,256]{1,2,0:T(8,128)S(1)} collective-permute-done((f32[1,256,256]{1,2,0:T(8,128)S(1)}, f32[1,256,256]{1,2,0:T(8,128)S(1)}, u32[]{:S(2)}, u32[]{:S(2)}) %collective-permute-start.1) | collective-permute-done | bytes 262176 | tf_op jit(solution)/shard_map/ppermute | solution.py:100
  210.3 1.8 multiply_reduce_fusion.3
  212.1 1.5 fusion.47
  214.5 2.6 fusion.41
  217.1 2.6 convolution_add_fusion.2
  219.9 2.5 fusion.142
  225.2 2.3 fusion.2
  230.7 53.4 %all-gather.7 = f32[8,4,256]{2,1,0:T(4,128)S(1)} all-gather(f32[1,4,256]{2,1,0:T(4,128)S(1)} %fusion.105), channel_id=7, replica_groups=mesh['ctx'=8,'probe'=4] {'ctx'}, dimensions={0}, use_global_device_ids=true | all-gather | bytes 36864 | tf_op jit(solution)/shard_map/all_gather | solution.py:13
  284.1 30.7 %all-gather.6 = f32[8,4,256]{2,1,0:T(4,128)S(1)} all-gather(f32[1,4,256]{2,1,0:T(4,128)S(1)} %bitcast.350), channel_id=5, replica_groups=mesh['ctx'=8,'probe'=4] {'ctx'}, dimensions={0}, use_global_device_ids=true | all-gather | bytes 36864 | tf_op jit(solution)/shard_map/all_gather | solution.py:13
  314.8 2.1 convolution_add_fusion.13
  316.9 2.4 fusion.15
  319.3 2.4 fusion.93
  321.7 3.1 fusion.20
  324.8 89.1 %all-gather.22.cloned.1.call-done = f32[32,256,256]{2,1,0:T(8,128)} async-done(((f32[4,256,256]{2,1,0:T(8,128)}), f32[32,256,256]{2,1,0:T(8,128)}) %all-gather.22.cloned.1.call-update) | async-done | bytes 8388624 | tf_op jit(solution)/shard_map/all_gather | solution.py:13
  415.0 26.3 %while.35 = (s32[]{:T(128)}, f32[1,256,256]{2,1,0:T(8,128)S(1)}, f32[4,256]{1,0:T(4,128)S(1)}, f32[4,256,256]{2,1,0:T(8,128)}, f32[4,256]{1,0:T(4,128)S(1)}, /*i...) while((s32[]{:T(128)}, f32[1,256,256]{2,1,0:T(8,128)S(1)}, ...), condition=%wide.region_14.15_spmd, body=%wide.region_13.14_spmd.sunk | while | flops 329734 | bytes 3956927 | solution.py:22
  415.0 2.7 bitcast_add_fusion.22
  418.7 2.7 bitcast_add_fusion.22
  422.5 2.7 bitcast_add_fusion.22
  426.2 2.7 bitcast_add_fusion.22
  429.9 2.7 bitcast_add_fusion.22
  433.6 2.7 bitcast_add_fusion.22
  437.3 2.7 bitcast_add_fusion.22
  442.0 3.7 fusion.11
  445.8 2.2 fusion.26
  450.0 2.4 fusion.92
  452.4 3.7 fusion.34
  456.1 3.6 fusion.1
  459.7 2.2 fusion
  468.6 2.0 multiply_reduce_fusion
  470.8 3.5 copy.230
  474.3 6.1 %psum.7 = f32[1,3,4]{2,1,0:T(4,128)S(1)} all-reduce(f32[1,3,4]{2,1,0:T(4,128)S(1)} %multiply_bitcast_fusion), channel_id=1, replica_groups=mesh['ctx'=8,'probe'=4] {'probe'}, use_global_device_ids=true, to_apply=%region_17.18 | all-reduce | flops 12 | bytes 96 | tf_op jit(solution)/shard_map/psum | solution.py:136
  (211 shorter events, 42.3 us)
Async XLA Ops:
  7.2 100.4 %all-gather.16.cloned.1.call-start = ((), (), s32[]{:S(2)}) async-start(), calls=%async_computation.1 | async-start | bytes 2359296 | tf_op jit(solution)/shard_map/all_gather | solution.py:13
  11.0 9.8 %copy-start.1 = (f32[1,256,1024]{1,2,0:T(8,128)}, f32[1,256,1024]{1,2,0:T(8,128)S(1)}, u32[]{:S(2)}) copy-start(f32[1,256,1024]{1,2,0:T(8,128)S(1)} %copy.182) | copy-start | bytes 3145732
  13.2 178.2 %all-gather.18.cloned.1.call-start = ((), (), s32[]{:S(2)}) async-start(), calls=%async_computation.2 | async-start | bytes 9437184 | tf_op jit(solution)/shard_map/all_gather | solution.py:13
  24.7 300.1 %all-gather.20.cloned.1.call-start = ((), (), s32[]{:S(2)}) async-start(), calls=%async_computation.3 | async-start | bytes 2359296 | tf_op jit(solution)/shard_map/all_gather | solution.py:13
  24.8 3.4 copy-start.25
  28.1 67.2 %copy-start.6 = (f32[1,256,1024]{1,2,0:T(8,128)}, f32[1,256,1024]{1,2,0:T(8,128)S(1)}, u32[]{:S(2)}) copy-start(f32[1,256,1024]{1,2,0:T(8,128)S(1)} %copy.283) | copy-start | bytes 3145732
  28.2 66.6 %copy-start.60 = (f32[4]{0:T(128)S(1)}, f32[4]{0:T(128)}, u32[]{:S(2)}) copy-start(f32[4]{0:T(128)} %param.10) | copy-start | bytes 52
  95.4 2.5 copy-start.35
  99.8 4.2 copy-start.26
  102.8 121.0 %copy-start.44 = (f32[4,256]{1,0:T(4,128)}, f32[4,256]{1,0:T(4,128)S(1)}, u32[]{:S(2)}) copy-start(f32[4,256]{1,0:T(4,128)S(1)} %get-tuple-element.294) | copy-start | bytes 12292
  102.8 2.6 copy-start.2
  193.3 4.2 copy-start.8
  193.3 8.9 %collective-permute-start = (f32[1,256,256]{1,2,0:T(8,128)}, f32[1,256,256]{1,2,0:T(8,128)S(1)}, u32[]{:S(2)}, u32[]{:S(2)}) collective-permute-start(f32[1,256,256]{1,2,0:T(8,128)} %copy.206), channel_id=1, source_target_pairs={{0,1},{1,2},{2,3},{3,0},{4,5},{5,6},{6,7},{7,4},{8,9},{9,10},{10,1... | collective-permute-start | bytes 786440 | tf_op jit(solution)/shard_map/ppermute | solution.py:100
  193.3 14.8 %collective-permute-start.2 = (f32[1,256,256]{1,2,0:T(8,128)}, f32[1,256,256]{1,2,0:T(8,128)S(1)}, u32[]{:S(2)}, u32[]{:S(2)}) collective-permute-start(f32[1,256,256]{1,2,0:T(8,128)} %copy.206), channel_id=1, source_target_pairs={{0,3},{1,0},{2,1},{3,2},{4,7},{5,4},{6,5},{7,6},{8,11},{9,8},{10,9... | collective-permute-start | bytes 786440 | tf_op jit(solution)/shard_map/ppermute | solution.py:102
  195.5 5.3 %copy-start.23 = (f32[256,4,256]{0,2,1:T(8,128)S(1)}, f32[256,4,256]{0,2,1:T(8,128)}, u32[]{:S(2)}) copy-start(f32[256,4,256]{0,2,1:T(8,128)} %select_add_fusion) | copy-start | bytes 3145732
  200.8 7.3 %copy-start.41 = (f32[1,256,256]{1,2,0:T(8,128)S(1)}, f32[1,256,256]{1,2,0:T(8,128)}, u32[]{:S(2)}) copy-start(f32[1,256,256]{1,2,0:T(8,128)} %copy.206) | copy-start | bytes 786436
  202.2 5.8 %collective-permute-start.1 = (f32[1,256,256]{1,2,0:T(8,128)S(1)}, f32[1,256,256]{1,2,0:T(8,128)S(1)}, u32[]{:S(2)}, u32[]{:S(2)}) collective-permute-start(f32[1,256,256]{1,2,0:T(8,128)S(1)} %collective-permute-done), channel_id=1, source_target_pairs={{0,1},{1,2},{2,3},{3,0},{4,5},{5,6},{6,7},{7,4},{8,9},{9,10},{10,1... | collective-permute-start | bytes 786440 | tf_op jit(solution)/shard_map/ppermute | solution.py:100
  202.3 14.7 %copy-start.48 = (f32[256,4]{0,1:T(4,128)}, f32[256,4]{0,1:T(4,128)S(1)}, u32[]{:S(2)}) copy-start(f32[256,4]{0,1:T(4,128)S(1)} %fusion.107) | copy-start | bytes 12292
  202.3 6.0 %copy-start.53 = (f32[4]{0:T(128)S(1)}, f32[4]{0:T(128)}, u32[]{:S(2)}) copy-start(f32[4]{0:T(128)} %get-tuple-element.336) | copy-start | bytes 52
  212.1 104.8 %copy-start.56 = (f32[256,4]{0,1:T(4,128)}, f32[256,4]{0,1:T(4,128)S(1)}, u32[]{:S(2)}) copy-start(f32[256,4]{0,1:T(4,128)S(1)} %get-tuple-element.352) | copy-start | bytes 12292
  214.4 199.5 %all-gather.22.cloned.1.call-start = ((), (), s32[]{:S(2)}) async-start(), calls=%async_computation.4 | async-start | bytes 9437184 | tf_op jit(solution)/shard_map/all_gather | solution.py:13
  214.4 2.6 copy-start.9
  219.6 236.5 %all-gather.14.cloned.1.call-start = ((), (), s32[]{:S(2)}) async-start(), calls=%async_computation | async-start | bytes 1310720 | tf_op jit(solution)/shard_map/all_gather | solution.py:120
  219.9 2.5 copy-start.3
  219.9 2.5 copy-start.30
  225.2 2.3 copy-start.10
  225.2 3.4 copy-start.24
  227.5 87.3 %copy-start.45 = (f32[4,256]{1,0:T(4,128)S(1)}, f32[4,256]{1,0:T(4,128)}, u32[]{:S(2)}) copy-start(f32[4,256]{1,0:T(4,128)} %copy-done.44) | copy-start | bytes 12292
  227.5 89.4 %copy-start.58 = (f32[4,256]{1,0:T(4,128)}, f32[4,256]{1,0:T(4,128)S(1)}, u32[]{:S(2)}) copy-start(f32[4,256]{1,0:T(4,128)S(1)} %get-tuple-element.349) | copy-start | bytes 12292
  316.9 4.8 copy-start.31
  316.9 2.4 copy-start.16
  319.3 2.4 copy-start.20
  442.0 3.8 copy-start.4
  442.0 3.8 copy-start.37
  442.0 3.8 copy-start.47
  442.0 3.8 copy-start.50
  442.0 3.8 copy-start.52
  445.8 2.2 copy-start.36
  450.0 2.4 copy-start.11
  450.0 2.4 copy-start.40
  450.0 2.4 copy-start.55
  450.0 2.4 copy-start.57
  450.0 2.4 copy-start.59
  452.4 3.7 copy-start.17
  456.1 3.6 copy-start
  459.7 2.2 copy-start.21
  459.7 2.2 copy-start.29
  466.5 2.2 copy-start.43
  (21 other events, 35.4 us)
Sparse Core Ops, SparseCore 0:
  13.3 52.3 all-gather.15
  67.8 123.5 all-gather.17
  214.5 73.7 all-gather.19
  290.3 123.4 all-gather.21
  442.1 13.9 all-gather.13
